TPU v7x, 512 devices: a whole 4x4x16 slice. The times are simulated.
512 devices in a mesh: dp: 8 (over x, core), expert: 64 (over y, z).
Axes of the slice: x: 4, y: 4, z: 16, core: 2. Of those that a mesh axis runs over, the one named last changes fastest.
Arguments:
- tokens: bfloat16 [65536, 1024], P(('dp', 'expert')), may hold values from -6 to 6
- grad_out: bfloat16 [65536, 1024], P(('dp', 'expert')), may hold values from -6 to 6
- expert_ids: int32 [65536, 8], P(('dp', 'expert')), may hold values from 0 to 63, all different within a row; in each aligned block of 128 rows (0 to 127, 128 to 255, ...) at most 18 rows name the same one
- gates: float32 [65536, 8], P(('dp', 'expert')), may hold values from 0.1 to 0.5
- w_in: bfloat16 [64, 1024, 768], P('expert', 'dp'), may hold values from -0.1875 to 0.1875
- w_down: bfloat16 [64, 384, 1024], P('expert', 'dp'), may hold values from -0.3125 to 0.3125
Outputs:
- grad_tokens: bfloat16 [65536, 1024], P(('dp', 'expert'))
- grad_in: float32 [64, 1024, 768], P('expert', 'dp')
- grad_down: float32 [64, 384, 1024], P('expert', 'dp')
Inputs may be any that keep to these rules, and one draw needn't show every extreme that they name: `expert_ids`: each token names 8 different experts; among the tokens of one device no expert is named more than 18 times, a bound that some block reaches.
All inputs are finite; a program needn't handle non-finite values.
Results may differ from a plain program's by a relative error of at most 0.015.
Values may be sent and summed in bfloat16 or wider, within the bound.
No kernel may reach another device: no remote copies, remote signals or barrier semaphores. Data moves between devices by JAX's collectives and lax.ppermute only.
A program may use at most 64 MiB of HBM per device.

v0:
```python
import jax
import jax.numpy as jnp
from jax import lax
from jax.sharding import PartitionSpec as P


def hidden_from(preact):
    half_width = preact.shape[1] // 2
    gate_pre = preact[:, :half_width]
    up_pre = preact[:, half_width:]
    sigmoid_gate = jax.nn.sigmoid(gate_pre)
    return (gate_pre * sigmoid_gate * up_pre).astype(jnp.bfloat16)


def pre_grads(preact, grad_hidden):
    half_width = preact.shape[1] // 2
    gate_pre = preact[:, :half_width]
    up_pre = preact[:, half_width:]
    sigmoid_gate = jax.nn.sigmoid(gate_pre)
    grad_gate = grad_hidden * up_pre * sigmoid_gate * (1.0 + gate_pre * (1.0 - sigmoid_gate))
    grad_up = grad_hidden * gate_pre * sigmoid_gate
    return jnp.concatenate([grad_gate, grad_up], axis=1).astype(jnp.bfloat16)


def contract_first(left, right):
    return lax.dot_general(
        left, right, (((0,), (0,)), ((), ())), preferred_element_type=jnp.float32
    )


def contract_last(left, right):
    return lax.dot_general(
        left, right, (((1,), (1,)), ((), ())), preferred_element_type=jnp.float32
    )


def expert_exchange(slots, expert_count):
    slot_total, chunks, lanes = slots.shape
    blocks = slots.reshape(expert_count, slot_total // expert_count * chunks, lanes)
    blocks = lax.all_to_all(blocks, "expert", 0, 0, tiled=True)
    return blocks.reshape(slot_total, chunks, lanes)


def on_device(tokens, grad_out, expert_ids, gates, w_in, w_down):
    token_rows, model_width = tokens.shape
    route_width = expert_ids.shape[1]
    expert_count = lax.axis_size("expert")
    route_total = token_rows * route_width
    capacity = route_total // expert_count + max(1, route_total // (8 * expert_count))
    slot_total = expert_count * capacity
    flat_ids = expert_ids.reshape(route_total)
    route_marks = (flat_ids[:, None] == jnp.arange(expert_count, dtype=jnp.int32)[None, :]).astype(
        jnp.int32
    )
    route_index = jnp.arange(route_total, dtype=jnp.int32)
    lower_table = (route_index[None, :] <= route_index[:, None]).astype(jnp.bfloat16)
    running = jnp.dot(
        lower_table, route_marks.astype(jnp.bfloat16), preferred_element_type=jnp.float32
    )
    slot_ranks = jnp.sum((running.astype(jnp.int32) - 1) * route_marks, axis=1)
    targets = flat_ids * capacity + slot_ranks
    slot_index = jnp.arange(slot_total, dtype=jnp.int32)
    slot_hits = slot_index[:, None] == targets[None, :]
    slot_gates = jnp.sum(jnp.where(slot_hits, gates.reshape(route_total)[None, :], 0.0), axis=1)
    token_of_route = (
        route_index[:, None] // route_width == jnp.arange(token_rows, dtype=jnp.int32)[None, :]
    ).astype(jnp.bfloat16)
    slot_of_token = jnp.dot(
        slot_hits.astype(jnp.bfloat16), token_of_route, preferred_element_type=jnp.float32
    ).astype(jnp.bfloat16)
    chunks = model_width // 128
    both_rows = jnp.concatenate(
        [tokens.reshape(token_rows, chunks, 128), grad_out.reshape(token_rows, chunks, 128)], axis=1
    )
    slot_routes = jnp.sum(jnp.where(slot_hits, route_index[None, :], 0), axis=1)
    occupied = jnp.any(slot_hits, axis=1)
    picked = both_rows[slot_routes // route_width].astype(jnp.float32)
    chunk_index = jnp.arange(2 * chunks, dtype=jnp.int32)[None, :, None]
    row_scale = jnp.where(
        chunk_index < chunks, jnp.ones((), jnp.float32), slot_gates[:, None, None]
    )
    row_scale = jnp.where(occupied[:, None, None], row_scale, jnp.zeros((), jnp.float32))
    send_both = (row_scale * picked).astype(jnp.bfloat16)
    recv_both = expert_exchange(send_both, expert_count)
    slot_tokens = recv_both[:, :chunks, :].reshape(slot_total, model_width)
    slot_grads = recv_both[:, chunks:, :].reshape(slot_total, model_width)
    local_in = w_in[0]
    local_down = w_down[0]
    full_in, full_down = (
        lax.all_gather(local_in, "dp", axis=0, tiled=True),
        lax.all_gather(local_down, "dp", axis=0, tiled=True),
    )
    preact = jnp.dot(slot_tokens, full_in, preferred_element_type=jnp.float32)
    grad_hidden = contract_last(slot_grads, full_down)
    pre_grad = pre_grads(preact, grad_hidden)
    slot_back = (
        contract_last(pre_grad, full_in).astype(jnp.bfloat16).reshape(slot_total, chunks, 128)
    )
    hidden_act = hidden_from(preact)
    grad_in_local = lax.psum_scatter(
        contract_first(slot_tokens, pre_grad).astype(jnp.bfloat16),
        "dp",
        scatter_dimension=0,
        tiled=True,
    ).astype(jnp.float32)
    grad_down_local = lax.psum_scatter(
        contract_first(hidden_act, slot_grads).astype(jnp.bfloat16),
        "dp",
        scatter_dimension=0,
        tiled=True,
    ).astype(jnp.float32)
    slot_return = expert_exchange(slot_back, expert_count)
    grad_tokens = (
        contract_first(slot_of_token, slot_return)
        .astype(jnp.bfloat16)
        .reshape(token_rows, model_width)
    )
    return (grad_tokens, grad_in_local[None], grad_down_local[None])


def solution(mesh):
    token_spec = P(("dp", "expert"), None)
    weight_spec = P("expert", "dp", None)
    in_specs = (token_spec, token_spec, token_spec, token_spec, weight_spec, weight_spec)
    out_specs = (token_spec, weight_spec, weight_spec)
    return jax.shard_map(
        on_device, mesh=mesh, in_specs=in_specs, out_specs=out_specs, check_vma=False
    )
```

profile of v0, /device:TPU:38, one launch (start us, length us, event | category | flops | bytes accessed | tf_op | source)
XLA Modules:
  0.0 400.0 jit_solution(4009378944013035038)
XLA Ops:
  7.2 0.8 copy.18
  10.2 0.8 copy.20
  12.7 4.8 %gather_fusion = bf16[1152,16,128]{2,1,0:T(8,128)(2,1)} fusion(bf16[128,16,128]{2,1,0:T(8,128)(2,1)S(1)} %pad_maximum_fusion.3, s32[2048]{0:T(1024)S(1)} %pad_clamp_fusion), kind=kCustom, calls=%fused_computation | custom fusion | bytes 9441792 | tf_op jit(solution)/shard_map/gather | solution.py:77
  17.5 6.3 %fusion = bf16[64,288,128]{2,1,0:T(8,128)(2,1)} fusion(f32[64,288]{1,0:T(8,128)S(1)} %copy.23, bf16[64,288,128]{2,1,0:T(8,128)(2,1)} %bitcast.56), kind=kLoop, calls=%fused_computation.2 | loop fusion | flops 7077888 | bytes 9510912 | tf_op jit(solution)/shard_map/convert_element_type | solution.py:83
  23.8 18.7 %all-to-all-start = ((bf16[64,288,128]{2,1,0:T(8,128)(2,1)}), bf16[64,288,128]{2,1,0:T(8,128)(2,1)}, u32[]{:S(2)}, u32[]{:S(2)}) async-start(bf16[64,288,128]{2,1,0:T(8,128)(2,1)} %fusion), calls=%async_computation | async-start | bytes 9437184 | tf_op jit(solution)/shard_map/all_to_all | solution.py:40
  43.2 13.6 %all-gather = bf16[1,384,1024]{2,1,0:T(8,128)(2,1)S(1)} all-gather(bf16[1,48,1024]{2,1,0:T(8,128)(2,1)S(1)} %copy-done.4), channel_id=2, replica_groups=mesh['dp'=8,'expert'=64] {'dp'}, dimensions={1}, use_global_device_ids=true | all-gather | bytes 884736 | tf_op jit(solution)/shard_map/all_gather | solution.py:91
  56.8 194.9 %all-to-all-done = bf16[64,288,128]{2,1,0:T(8,128)(2,1)} async-done(((bf16[64,288,128]{2,1,0:T(8,128)(2,1)}), bf16[64,288,128]{2,1,0:T(8,128)(2,1)}, u32[]{:S(2)}, u32[]{:S(2)}) %all-to-all-start) | async-done | bytes 4718624 | tf_op jit(solution)/shard_map/all_to_all | solution.py:40
  251.7 3.6 fusion.44
  255.4 4.7 %fusion.7 = f32[1152,768]{0,1:T(8,128)S(1)} fusion(bf16[144,8,8,128]{3,2,1,0:T(8,128)(2,1)S(1)} %bitcast.59, bf16[1,1024,768]{2,1,0:T(8,128)(2,1)} %all-gather.4.cloned.1.call-done), kind=kOutput, calls=%fused_computation.14 | convolution fusion | flops 1811939328 | bytes 7471104 | tf_op jit(solution)/shard_map/dot_general | solution.py:93
  260.1 1.7 multiply_convert_fusion.2
  261.9 0.9 copy-done.7
  263.1 2.1 convolution_convert_fusion
  265.1 2.5 reshape_reshape.3
  267.6 8.7 %all-to-all-start.1 = ((bf16[64,144,128]{2,1,0:T(8,128)(2,1)}), bf16[64,144,128]{2,1,0:T(8,128)(2,1)S(1)}, u32[]{:S(2)}, u32[]{:S(2)}) async-start(bf16[64,144,128]{2,1,0:T(8,128)(2,1)} %reshape_reshape.3), calls=%async_computation.1 | async-start | bytes 4718592 | tf_op jit(solution)/shard_map/all_to_all | solution.py:40
  276.3 4.9 %fusion.23 = bf16[384,1024]{1,0:T(8,128)(2,1)} fusion(bf16[144,8,8,128]{3,2,1,0:T(8,128)(2,1)} %bitcast.61, f32[1152,768]{0,1:T(8,128)} %copy-done.6), kind=kOutput, calls=%fused_computation.33 | convolution fusion | flops 909017088 | bytes 6684672 | tf_op jit(solution)/shard_map/dot_general | solution.py:26
  281.6 5.6 %fusion.18 = bf16[1024,768]{1,0:T(8,128)(2,1)} fusion(bf16[144,8,8,128]{3,2,1,0:T(8,128)(2,1)} %bitcast.60, bf16[1152,384]{0,1:T(8,128)(2,1)} %copy-done.8, bf16[1152,384]{0,1:T(8,128)(2,1)} %copy-done.7), kind=kOutput, calls=%fused_computation.30 | convolution fusion | flops 1816264704 | bytes 5701632 | tf_op jit(solution)/shard_map/dot_general | solution.py:26
  287.1 31.9 %reduce-scatter.5.cloned.1.call-done = bf16[48,1024]{1,0:T(8,128)(2,1)} async-done(((bf16[384,1024]{1,0:T(8,128)(2,1)}), bf16[48,1024]{1,0:T(8,128)(2,1)}) %reduce-scatter.5.cloned.1.call-update) | async-done | bytes 98320 | tf_op jit(solution)/shard_map/reduce_scatter | solution.py:106
  319.0 1.6 bitcast_convert_fusion.1
  320.6 41.5 %reduce-scatter.3.cloned.1.call-done = bf16[128,768]{1,0:T(8,128)(2,1)} async-done(((bf16[1024,768]{1,0:T(8,128)(2,1)}), bf16[128,768]{1,0:T(8,128)(2,1)}) %reduce-scatter.3.cloned.1.call-update) | async-done | bytes 196624 | tf_op jit(solution)/shard_map/reduce_scatter | solution.py:100
  362.1 1.7 bitcast_convert_fusion
  363.8 21.8 %all-to-all-done.1 = bf16[64,144,128]{2,1,0:T(8,128)(2,1)S(1)} async-done(((bf16[64,144,128]{2,1,0:T(8,128)(2,1)}), bf16[64,144,128]{2,1,0:T(8,128)(2,1)S(1)}, u32[]{:S(2)}, u32[]{:S(2)}) %all-to-all-start.1) | async-done | bytes 2359328 | tf_op jit(solution)/shard_map/all_to_all | solution.py:40
  385.6 2.8 copy.24
  388.3 4.2 %fusion.26 = f32[128,1024]{0,1:S(1)} fusion(bf16[1152,1024]{0,1:T(8,128)(2,1)} %bitcast.58, s32[1024]{0:T(1024)S(1)} %get-tuple-element.17, s32[1024]{0:T(1024)S(1)} %get-tuple-element.16), kind=kOutput, calls=%fused_computation.34 | convolution fusion | flops 605437952 | bytes 2891776
  392.6 0.9 copy.25
  (47 shorter events, 5.3 us)
Async XLA Ops:
  7.2 5.3 %copy-start.2 = (bf16[128,1024]{1,0:T(8,128)(2,1)S(1)}, bf16[128,1024]{1,0:T(8,128)(2,1)}, u32[]{:S(2)}) copy-start(bf16[128,1024]{1,0:T(8,128)(2,1)} %param.6) | copy-start | bytes 786436
  7.2 5.4 %copy-start.3 = (bf16[128,1024]{1,0:T(8,128)(2,1)S(1)}, bf16[128,1024]{1,0:T(8,128)(2,1)}, u32[]{:S(2)}) copy-start(bf16[128,1024]{1,0:T(8,128)(2,1)} %param.7) | copy-start | bytes 786436
  23.8 19.4 %copy-start.4 = (bf16[1,48,1024]{2,1,0:T(8,128)(2,1)S(1)}, bf16[1,48,1024]{2,1,0:T(8,128)(2,1)}, u32[]{:S(2)}) copy-start(bf16[1,48,1024]{2,1,0:T(8,128)(2,1)} %param.11) | copy-start | bytes 294916
  23.8 227.9 %all-to-all-start = ((bf16[64,288,128]{2,1,0:T(8,128)(2,1)}), bf16[64,288,128]{2,1,0:T(8,128)(2,1)}, u32[]{:S(2)}, u32[]{:S(2)}) async-start(bf16[64,288,128]{2,1,0:T(8,128)(2,1)} %fusion), calls=%async_computation | async-start | bytes 9437184 | tf_op jit(solution)/shard_map/all_to_all | solution.py:40
  42.5 212.9 %all-gather.4.cloned.1.call-start = ((), (), s32[]{:S(2)}) async-start(), calls=%async_computation.6 | async-start | bytes 1769472 | tf_op jit(solution)/shard_map/all_gather | solution.py:90
  255.3 4.7 %copy-start = (bf16[1152,8,128]{2,1,0:T(8,128)(2,1)}, bf16[1152,8,128]{2,1,0:T(8,128)(2,1)S(1)}, u32[]{:S(2)}) copy-start(bf16[1152,8,128]{2,1,0:T(8,128)(2,1)S(1)} %get-tuple-element.14) | copy-start | bytes 7077892
  255.4 4.7 %copy-start.1 = (bf16[1152,8,128]{2,1,0:T(8,128)(2,1)S(1)}, bf16[1152,8,128]{2,1,0:T(8,128)(2,1)}, u32[]{:S(2)}) copy-start(bf16[1152,8,128]{2,1,0:T(8,128)(2,1)} %get-tuple-element.15) | copy-start | bytes 7077892
  260.0 1.8 copy-start.6
  260.1 3.0 copy-start.5
  261.9 0.9 copy-start.7
  261.9 1.2 copy-start.8
  267.6 117.9 %all-to-all-start.1 = ((bf16[64,144,128]{2,1,0:T(8,128)(2,1)}), bf16[64,144,128]{2,1,0:T(8,128)(2,1)S(1)}, u32[]{:S(2)}, u32[]{:S(2)}) async-start(bf16[64,144,128]{2,1,0:T(8,128)(2,1)} %reshape_reshape.3), calls=%async_computation.1 | async-start | bytes 4718592 | tf_op jit(solution)/shard_map/all_to_all | solution.py:40
  276.3 42.7 %reduce-scatter.5.cloned.1.call-start = ((), (), s32[]{:S(2)}) async-start(), calls=%async_computation.5 | async-start | bytes 884736 | tf_op jit(solution)/shard_map/reduce_scatter | solution.py:106
  281.3 80.8 %reduce-scatter.3.cloned.1.call-start = ((), (), s32[]{:S(2)}) async-start(), calls=%async_computation.4 | async-start | bytes 1769472 | tf_op jit(solution)/shard_map/reduce_scatter | solution.py:100
Sparse Core Ops, SparseCore 0:
  45.4 31.1 all-gather.3
  281.4 37.5 reduce-scatter.4
  321.9 40.1 reduce-scatter.2
where the time goes:
time: 400 us
  waiting for transfers between devices  291 us (73%)
  starting transfers between devices  27.7 us (7%)
  matrix products  23.7 us (6%)
  local copies, waits for them, and re-layouts  18.8 us (5%)
  between operations  14 us (4%)
  blocking collectives  13.6 us (3%)
  other arithmetic  11.5 us (3%)
    all_to_all x2, waiting for transfers between devices, expert_exchange(): blocks = lax.all_to_all(blocks, 'expert', 0, 0, tiled=True)  217 us
    reduce_scatter x1, waiting for transfers between devices, on_device(): lax.psum_scatter(contract_first(slot_tokens, pre_grad).astype(jnp.bfloat1...  41.5 us
    reduce_scatter x1, waiting for transfers between devices, on_device(): lax.psum_scatter(contract_first(hidden_act, slot_grads).astype(jnp.bfloat...  31.9 us
    all_to_all x2, starting transfers between devices, expert_exchange(): blocks = lax.all_to_all(blocks, 'expert', 0, 0, tiled=True)  27.3 us
    all_gather x1, blocking collectives, on_device(): lax.all_gather(local_down, 'dp', axis=0, tiled=True)  13.6 us
    dot_general x2, matrix products, contract_first(): lax.dot_general(left, right, (((0,), (0,)), ((), ())), preferred_element_...  10.5 us
  transfers between devices with their start and end apart: 5, of which 4 were waited for; matrix products, arithmetic and copies ran while one was open for 4% of the time, Pallas kernels for 0%

commit v1 on v0

--- a/solution.py
+++ b/solution.py
@@ -42,6 +42,16 @@
 
 
 def on_device(tokens, grad_out, expert_ids, gates, w_in, w_down):
+
+    def attach_counts(values, net_axis, axis_no):
+        return lax.all_to_all(
+            jnp.concatenate(tuple((values for _ in range(lax.axis_size(net_axis)))), axis=axis_no),
+            net_axis,
+            axis_no,
+            axis_no,
+            tiled=True,
+        )
+
     token_rows, model_width = tokens.shape
     route_width = expert_ids.shape[1]
     expert_count = lax.axis_size("expert")
@@ -88,7 +98,7 @@
     local_down = w_down[0]
     full_in, full_down = (
         lax.all_gather(local_in, "dp", axis=0, tiled=True),
-        lax.all_gather(local_down, "dp", axis=0, tiled=True),
+        attach_counts(local_down, "dp", axis_no=0),
     )
     preact = jnp.dot(slot_tokens, full_in, preferred_element_type=jnp.float32)
     grad_hidden = contract_last(slot_grads, full_down)

time: 400 us -> 412 us (1.030)
  the two profiles are of different devices: /device:TPU:38 before, /device:TPU:32 now
where the time goes in v1:
time: 412 us; the launch traced here: 411 us
  waiting for transfers between devices  302 us (73%)
  starting transfers between devices  32 us (8%)
  matrix products  28.1 us (7%)
  local copies, waits for them, and re-layouts  23.8 us (6%)
  between operations  13.9 us (3%)
  other arithmetic  11.5 us (3%)
    all_to_all x2, waiting for transfers between devices, expert_exchange(): blocks = lax.all_to_all(blocks, 'expert', 0, 0, tiled=True)  223 us
    reduce_scatter x1, waiting for transfers between devices, on_device(): lax.psum_scatter(contract_first(slot_tokens, pre_grad).astype(jnp.bfloat1...  41.7 us
    reduce_scatter x1, waiting for transfers between devices, on_device(): lax.psum_scatter(contract_first(hidden_act, slot_grads).astype(jnp.bfloat...  33.1 us
    all_to_all x2, starting transfers between devices, expert_exchange(): blocks = lax.all_to_all(blocks, 'expert', 0, 0, tiled=True)  27.3 us
    dot_general x2, matrix products, contract_first(): lax.dot_general(left, right, (((0,), (0,)), ((), ())), preferred_element_...  10.4 us
    unnamed x26, local copies, waits for them, and re-layouts  8.34 us
  transfers between devices with their start and end apart: 6, of which 5 were waited for; matrix products, arithmetic and copies ran while one was open for 7% of the time, Pallas kernels for 0%

profile of v1, /device:TPU:32, one launch (start us, length us, event | category | flops | bytes accessed | tf_op | source)
XLA Modules:
  0.0 411.4 jit_solution(5260838658396329920)
XLA Ops:
  7.2 0.8 copy.18
  12.7 4.8 %gather_fusion = bf16[1152,16,128]{2,1,0:T(8,128)(2,1)} fusion(bf16[128,16,128]{2,1,0:T(8,128)(2,1)S(1)} %pad_maximum_fusion.3, s32[2048]{0:T(1024)S(1)} %pad_clamp_fusion), kind=kCustom, calls=%fused_computation | custom fusion | bytes 9441792 | tf_op jit(solution)/shard_map/gather | solution.py:87
  17.5 6.2 %fusion = bf16[64,288,128]{2,1,0:T(8,128)(2,1)} fusion(f32[64,288]{1,0:T(8,128)S(1)} %copy.23, bf16[64,288,128]{2,1,0:T(8,128)(2,1)} %bitcast.63), kind=kLoop, calls=%fused_computation.2 | loop fusion | flops 7077888 | bytes 9510912 | tf_op jit(solution)/shard_map/convert_element_type | solution.py:93
  23.8 18.7 %all-to-all-start = ((bf16[64,288,128]{2,1,0:T(8,128)(2,1)}), bf16[64,288,128]{2,1,0:T(8,128)(2,1)}, u32[]{:S(2)}, u32[]{:S(2)}) async-start(bf16[64,288,128]{2,1,0:T(8,128)(2,1)} %fusion), calls=%async_computation | async-start | bytes 9437184 | tf_op jit(solution)/shard_map/all_to_all | solution.py:40
  48.4 203.3 %all-to-all-done = bf16[64,288,128]{2,1,0:T(8,128)(2,1)} async-done(((bf16[64,288,128]{2,1,0:T(8,128)(2,1)}), bf16[64,288,128]{2,1,0:T(8,128)(2,1)}, u32[]{:S(2)}, u32[]{:S(2)}) %all-to-all-start) | async-done | bytes 4718624 | tf_op jit(solution)/shard_map/all_to_all | solution.py:40
  251.7 4.3 %all-to-all-start.1 = ((bf16[8,48,1024]{2,1,0:T(8,128)(2,1)}), bf16[8,48,1024]{2,1,0:T(8,128)(2,1)S(1)}, u32[]{:S(2)}, u32[]{:S(2)}) async-start(bf16[8,48,1024]{2,1,0:T(8,128)(2,1)} %bitcast.5), calls=%async_computation.1 | async-start | bytes 1572864 | tf_op jit(solution)/shard_map/all_to_all | solution.py:47
  256.0 3.6 fusion.43
  259.6 6.4 %fusion.7 = f32[1152,768]{0,1:T(8,128)} fusion(bf16[144,8,8,128]{3,2,1,0:T(8,128)(2,1)S(1)} %bitcast.66, bf16[1,1024,768]{2,1,0:T(8,128)(2,1)} %all-gather.3.cloned.1.call-done), kind=kOutput, calls=%fused_computation.14 | convolution fusion | flops 1811939328 | bytes 7471104 | tf_op jit(solution)/shard_map/dot_general | solution.py:103
  266.1 3.1 all-to-all-done.1
  269.2 4.4 %multiply_convert_fusion.2 = (bf16[1152,384]{0,1:T(8,128)(2,1)S(1)}, bf16[1152,384]{0,1:T(8,128)(2,1)S(1)}) fusion(f32[1152,768]{0,1:T(8,128)} %fusion.7, bf16[384,1024]{1,0:T(8,128)(2,1)S(1)} %bitcast.73, bf16[144,8,8,128]{3,2,1,0:T(8,128)(2,1)} %bitcast.68), kind=kOutput, calls=%fused_computation.28 | convolution fusion | flops 911720448 | bytes 8454144 | tf_op jit(solution)/shard_map/dot_general | solution.py:32
  273.6 0.9 copy-done.5
  274.8 2.0 convolution_convert_fusion
  276.9 2.5 reshape_reshape.3
  279.4 8.7 %all-to-all-start.2 = ((bf16[64,144,128]{2,1,0:T(8,128)(2,1)}), bf16[64,144,128]{2,1,0:T(8,128)(2,1)S(1)}, u32[]{:S(2)}, u32[]{:S(2)}) async-start(bf16[64,144,128]{2,1,0:T(8,128)(2,1)} %reshape_reshape.3), calls=%async_computation.2 | async-start | bytes 4718592 | tf_op jit(solution)/shard_map/all_to_all | solution.py:40
  288.1 4.9 %fusion.23 = bf16[384,1024]{1,0:T(8,128)(2,1)} fusion(bf16[144,8,8,128]{3,2,1,0:T(8,128)(2,1)} %bitcast.69, f32[1152,768]{0,1:T(8,128)} %fusion.7), kind=kOutput, calls=%fused_computation.33 | convolution fusion | flops 909017088 | bytes 6684672 | tf_op jit(solution)/shard_map/dot_general | solution.py:26
  293.2 5.6 %fusion.18 = bf16[1024,768]{1,0:T(8,128)(2,1)} fusion(bf16[144,8,8,128]{3,2,1,0:T(8,128)(2,1)} %bitcast.67, bf16[1152,384]{0,1:T(8,128)(2,1)} %copy-done.6, bf16[1152,384]{0,1:T(8,128)(2,1)} %copy-done.5), kind=kOutput, calls=%fused_computation.30 | convolution fusion | flops 1816264704 | bytes 5701632 | tf_op jit(solution)/shard_map/dot_general | solution.py:26
  298.8 33.1 %reduce-scatter.5.cloned.1.call-done = bf16[48,1024]{1,0:T(8,128)(2,1)} async-done(((bf16[384,1024]{1,0:T(8,128)(2,1)}), bf16[48,1024]{1,0:T(8,128)(2,1)}) %reduce-scatter.5.cloned.1.call-update) | async-done | bytes 98320 | tf_op jit(solution)/shard_map/reduce_scatter | solution.py:116
  331.9 1.6 bitcast_convert_fusion.1
  333.5 41.7 %reduce-scatter.3.cloned.1.call-done = bf16[128,768]{1,0:T(8,128)(2,1)} async-done(((bf16[1024,768]{1,0:T(8,128)(2,1)}), bf16[128,768]{1,0:T(8,128)(2,1)}) %reduce-scatter.3.cloned.1.call-update) | async-done | bytes 196624 | tf_op jit(solution)/shard_map/reduce_scatter | solution.py:110
  375.3 1.7 bitcast_convert_fusion
  377.0 20.0 %all-to-all-done.2 = bf16[64,144,128]{2,1,0:T(8,128)(2,1)S(1)} async-done(((bf16[64,144,128]{2,1,0:T(8,128)(2,1)}), bf16[64,144,128]{2,1,0:T(8,128)(2,1)S(1)}, u32[]{:S(2)}, u32[]{:S(2)}) %all-to-all-start.2) | async-done | bytes 2359328 | tf_op jit(solution)/shard_map/all_to_all | solution.py:40
  397.0 2.8 copy.24
  399.7 4.2 %fusion.26 = f32[128,1024]{0,1:S(1)} fusion(bf16[1152,1024]{0,1:T(8,128)(2,1)} %bitcast.65, s32[1024]{0:T(1024)S(1)} %get-tuple-element.17, s32[1024]{0:T(1024)S(1)} %get-tuple-element.16), kind=kOutput, calls=%fused_computation.34 | convolution fusion | flops 605437952 | bytes 2891776
  404.0 0.9 copy.25
  (52 shorter events, 11.2 us)
Async XLA Ops:
  7.2 5.3 %copy-start.2 = (bf16[128,1024]{1,0:T(8,128)(2,1)S(1)}, bf16[128,1024]{1,0:T(8,128)(2,1)}, u32[]{:S(2)}) copy-start(bf16[128,1024]{1,0:T(8,128)(2,1)} %param.6) | copy-start | bytes 786436
  7.2 5.4 %copy-start.3 = (bf16[128,1024]{1,0:T(8,128)(2,1)S(1)}, bf16[128,1024]{1,0:T(8,128)(2,1)}, u32[]{:S(2)}) copy-start(bf16[128,1024]{1,0:T(8,128)(2,1)} %param.7) | copy-start | bytes 786436
  23.8 19.4 %copy-start = (bf16[1,48,1024]{2,1,0:T(8,128)(2,1)S(1)}, bf16[1,48,1024]{2,1,0:T(8,128)(2,1)}, u32[]{:S(2)}) copy-start(bf16[1,48,1024]{2,1,0:T(8,128)(2,1)} %param.11) | copy-start | bytes 294916
  23.8 227.9 %all-to-all-start = ((bf16[64,288,128]{2,1,0:T(8,128)(2,1)}), bf16[64,288,128]{2,1,0:T(8,128)(2,1)}, u32[]{:S(2)}, u32[]{:S(2)}) async-start(bf16[64,288,128]{2,1,0:T(8,128)(2,1)} %fusion), calls=%async_computation | async-start | bytes 9437184 | tf_op jit(solution)/shard_map/all_to_all | solution.py:40
  42.5 217.2 %all-gather.3.cloned.1.call-start = ((), (), s32[]{:S(2)}) async-start(), calls=%async_computation.7 | async-start | bytes 1769472 | tf_op jit(solution)/shard_map/all_gather | solution.py:100
  251.7 17.4 %all-to-all-start.1 = ((bf16[8,48,1024]{2,1,0:T(8,128)(2,1)}), bf16[8,48,1024]{2,1,0:T(8,128)(2,1)S(1)}, u32[]{:S(2)}, u32[]{:S(2)}) async-start(bf16[8,48,1024]{2,1,0:T(8,128)(2,1)} %bitcast.5), calls=%async_computation.1 | async-start | bytes 1572864 | tf_op jit(solution)/shard_map/all_to_all | solution.py:47
  259.6 6.4 %copy-start.1 = (bf16[1152,8,128]{2,1,0:T(8,128)(2,1)}, bf16[1152,8,128]{2,1,0:T(8,128)(2,1)S(1)}, u32[]{:S(2)}) copy-start(bf16[1152,8,128]{2,1,0:T(8,128)(2,1)S(1)} %get-tuple-element.14) | copy-start | bytes 7077892
  269.2 5.7 %copy-start.4 = (bf16[1,1024,768]{2,1,0:T(8,128)(2,1)S(1)}, bf16[1,1024,768]{2,1,0:T(8,128)(2,1)}, u32[]{:S(2)}) copy-start(bf16[1,1024,768]{2,1,0:T(8,128)(2,1)} %all-gather.3.cloned.1.call-done) | copy-start | bytes 4718596
  273.6 0.9 copy-start.5
  273.6 1.2 copy-start.6
  279.4 117.6 %all-to-all-start.2 = ((bf16[64,144,128]{2,1,0:T(8,128)(2,1)}), bf16[64,144,128]{2,1,0:T(8,128)(2,1)S(1)}, u32[]{:S(2)}, u32[]{:S(2)}) async-start(bf16[64,144,128]{2,1,0:T(8,128)(2,1)} %reshape_reshape.3), calls=%async_computation.2 | async-start | bytes 4718592 | tf_op jit(solution)/shard_map/all_to_all | solution.py:40
  288.0 43.9 %reduce-scatter.5.cloned.1.call-start = ((), (), s32[]{:S(2)}) async-start(), calls=%async_computation.6 | async-start | bytes 884736 | tf_op jit(solution)/shard_map/reduce_scatter | solution.py:116
  293.0 82.3 %reduce-scatter.3.cloned.1.call-start = ((), (), s32[]{:S(2)}) async-start(), calls=%async_computation.5 | async-start | bytes 1769472 | tf_op jit(solution)/shard_map/reduce_scatter | solution.py:110
Sparse Core Ops, SparseCore 0:
  45.4 32.7 all-gather.2
  293.1 38.8 reduce-scatter.4
  334.8 40.4 reduce-scatter.2
